TPU v7x, 512 devices: a whole 4x4x16 slice. The times are simulated.
512 devices in a mesh: dp: 8 (over x, core), expert: 64 (over y, z).
Axes of the slice: x: 4, y: 4, z: 16, core: 2. Of those that a mesh axis runs over, the one named last changes fastest.
Arguments:
- query_rows: bfloat16 [65536, 2048], P(('dp', 'expert')), may hold values from -40 to 40
- key_rows: bfloat16 [65536, 256], P(('dp', 'expert')), may hold values from -40 to 40
- value_rows: bfloat16 [65536, 256], P(('dp', 'expert')), may hold values from -6 to 6
- residual: bfloat16 [65536, 1024], P(('dp', 'expert')), may hold values from -25 to 25
- document_owner: int32 [512, 8], P(('dp', 'expert')), may hold values from 0 to 7, as said below
- document_length: int32 [512, 8], P(('dp', 'expert')), may hold values from 8 to 24, as said below
- document_offset: int32 [512, 8], P(('dp', 'expert')), may hold values from 0 to 120, as said below
- query_gain: float32 [128], replicated, may hold values from 0.3 to 5.5
- key_gain: float32 [128], replicated, may hold values from 0.3 to 5.5
- output_weight: bfloat16 [2048, 1024], P('expert'), may hold values from -0.125 to 0.125
- post_gain: float32 [1024], replicated, may hold values from 0.5 to 2
- routes: int32 [65536, 8], P(('dp', 'expert')), may hold values from 0 to 63, all different within a row; in each aligned block of 128 rows (0 to 127, 128 to 255, ...) at most 20 rows name the same one
- route_weight: float32 [65536, 8], P(('dp', 'expert')), may hold values from 0.1 to 1
- gate_weight: bfloat16 [64, 768, 1024], P('expert', 'dp'), may hold values from -0.1875 to 0.1875
- up_weight: bfloat16 [64, 768, 1024], P('expert', 'dp'), may hold values from -0.1875 to 0.1875
- down_weight: bfloat16 [64, 768, 1024], P('expert', 'dp'), may hold values from -0.21875 to 0.21875
Outputs:
- layer_out: bfloat16 [65536, 1024], P(('dp', 'expert'))
Inputs may be any that keep to these rules, and one draw needn't show every extreme that they name: `document_owner`: each device's row names every dp index once, so a device sends exactly one document to each pack owner of its expert column. `document_length`: A device's lengths sum to 128; the documents that all devices of an expert column send to one owner also sum to 128; no device sends more than 24 rows to one owner, and some device does in every column. `document_offset`: the documents that reach one owner cover its 128 pack rows exactly once. `routes`: at most 20 of one device's rows name one expert; a row names 8 different experts.
All inputs are finite; a program needn't handle non-finite values.
Results may differ from a plain program's by a relative error of at most 0.012.
The roundings to bfloat16 on the way count: a program that leaves them out, or rounds other values in their place, can miss the bound.
Values may be sent and summed in bfloat16 or wider, within the bound.
No kernel may reach another device: no remote copies, remote signals or barrier semaphores. Data moves between devices by JAX's collectives and lax.ppermute only.
A program may use at most 64 MiB of HBM per device.

v0:
```python
import jax
import jax.numpy as jnp
from jax import lax
from jax.sharding import PartitionSpec as P

norm_epsilon = 1e-06
rope_base = 1000000.0


def rms_scale(values, gain):
    mean_square = jnp.mean(values * values, axis=-1, keepdims=True)
    return values * lax.rsqrt(mean_square + norm_epsilon) * gain


def rotary(values, positions):
    head_width = values.shape[-1]
    half_width = head_width // 2
    frequency = rope_base ** (-2.0 * jnp.arange(half_width, dtype=jnp.float32) / head_width)
    angles = positions.astype(jnp.float32)[:, None] * frequency[None, :]
    cosine_part = jnp.cos(angles)[:, None, :]
    sine_part = jnp.sin(angles)[:, None, :]
    leading = values[..., :half_width]
    trailing = values[..., half_width:]
    return jnp.concatenate(
        [
            leading * cosine_part - trailing * sine_part,
            trailing * cosine_part + leading * sine_part,
        ],
        axis=-1,
    )


def attend(query_part, key_part, value_part, identity, position, query_gain, key_gain):
    row_total = query_part.shape[0]
    head_width = query_gain.shape[0]
    head_count = query_part.shape[1] // head_width
    key_heads = key_part.shape[1] // head_width
    group_size = head_count // key_heads
    queries = rotary(
        rms_scale(
            query_part.reshape(row_total, head_count, head_width).astype(jnp.float32), query_gain
        ),
        position,
    ).astype(jnp.bfloat16)
    keys_normed = rotary(
        rms_scale(key_part.reshape(row_total, key_heads, head_width).astype(jnp.float32), key_gain),
        position,
    ).astype(jnp.bfloat16)
    queries = queries.reshape(row_total, key_heads, group_size, head_width)
    scores = jnp.einsum(
        "pkgd,qkd->kgpq", queries, keys_normed, preferred_element_type=jnp.float32
    ) * head_width ** (-0.5)
    allowed = (identity[:, None] == identity[None, :]) & (position[None, :] <= position[:, None])
    scores = jnp.where(allowed, scores, -jnp.inf)
    largest = jnp.max(scores, axis=-1, keepdims=True)
    powers = jnp.exp(scores - largest)
    weights = (powers / jnp.sum(powers, axis=-1, keepdims=True)).astype(jnp.bfloat16)
    values_heads = value_part.reshape(row_total, key_heads, head_width)
    mixed = jnp.einsum("kgpq,qkd->pkgd", weights, values_heads, preferred_element_type=jnp.float32)
    return mixed.astype(jnp.bfloat16).reshape(row_total, head_count * head_width)


def project_heads(attended, output_weight):
    return jnp.dot(
        attended,
        lax.all_gather(output_weight, "expert", axis=0, tiled=True),
        preferred_element_type=jnp.float32,
    )


def hidden_product(block, gate_part, up_part, down_part):
    contract = (((1,), (1,)), ((), ()))
    gate_value = lax.dot_general(block, gate_part, contract, preferred_element_type=jnp.float32)
    up_value = lax.dot_general(block, up_part, contract, preferred_element_type=jnp.float32)
    active = (jax.nn.silu(gate_value) * up_value).astype(jnp.bfloat16)
    return jnp.dot(active, down_part, preferred_element_type=jnp.float32)


def expert_output(work_rows, gate_part, up_part, down_part):
    return hidden_product(work_rows, gate_part, up_part, down_part)


def local(
    query_rows,
    key_rows,
    value_rows,
    residual,
    document_owner,
    document_length,
    document_offset,
    query_gain,
    key_gain,
    output_weight,
    post_gain,
    routes,
    route_weight,
    gate_weight,
    up_weight,
    down_weight,
):
    owner_total = lax.axis_size("dp")
    expert_total = lax.axis_size("expert")
    row_total = query_rows.shape[0]
    capacity = row_total * 3 // (2 * owner_total)
    owners = document_owner[0]
    lengths = document_length[0]
    offsets = document_offset[0]
    starts = jnp.cumsum(lengths) - lengths
    owner_ids = jnp.arange(owner_total, dtype=jnp.int32)
    matches = owners[None, :] == owner_ids[:, None]
    start_of = jnp.sum(jnp.where(matches, starts[None, :], 0), axis=1)
    length_of = jnp.sum(jnp.where(matches, lengths[None, :], 0), axis=1)
    offset_of = jnp.sum(jnp.where(matches, offsets[None, :], 0), axis=1)
    slot_ids = jnp.arange(capacity, dtype=jnp.int32)
    source_rows = jnp.minimum(start_of[:, None] + slot_ids[None, :], row_total - 1).reshape(-1)
    pack_slot = jnp.where(
        slot_ids[None, :] < length_of[:, None], offset_of[:, None] + slot_ids[None, :], -1
    )
    total_slots = owner_total * capacity
    flat_slots = jnp.arange(total_slots, dtype=jnp.int32)
    pack_ids = jnp.arange(row_total, dtype=jnp.int32)
    got_query, got_key, got_value, got_residual, got_slot = (
        lax.all_to_all(
            query_rows[source_rows].reshape(owner_total, capacity, -1),
            "dp",
            split_axis=0,
            concat_axis=0,
            tiled=True,
        ),
        lax.all_to_all(
            key_rows[source_rows].reshape(owner_total, capacity, -1),
            "dp",
            split_axis=0,
            concat_axis=0,
            tiled=True,
        ),
        lax.all_to_all(
            value_rows[source_rows].reshape(owner_total, capacity, -1),
            "dp",
            split_axis=0,
            concat_axis=0,
            tiled=True,
        ),
        lax.all_to_all(
            residual[source_rows].reshape(owner_total, capacity, -1),
            "dp",
            split_axis=0,
            concat_axis=0,
            tiled=True,
        ),
        lax.all_to_all(pack_slot, "dp", split_axis=0, concat_axis=0, tiled=True),
    )
    placed = got_slot.reshape(-1)[None, :] == pack_ids[:, None]
    slot_of = jnp.sum(jnp.where(placed, flat_slots[None, :], 0), axis=1)
    pack_query = got_query.reshape(total_slots, -1)[slot_of]
    pack_key = got_key.reshape(total_slots, -1)[slot_of]
    pack_value = got_value.reshape(total_slots, -1)[slot_of]
    pack_residual = got_residual.reshape(total_slots, -1)[slot_of]
    identity = slot_of // capacity
    position = slot_of % capacity
    attended = attend(pack_query, pack_key, pack_value, identity, position, query_gain, key_gain)
    hidden_state = pack_residual.astype(jnp.float32) + project_heads(attended, output_weight)
    normed = rms_scale(hidden_state, post_gain).astype(jnp.bfloat16)
    top_total = routes.shape[1]
    most = row_total * top_total * 5 // (4 * expert_total)
    expert_ids = jnp.arange(expert_total, dtype=jnp.int32)
    routed = routes[:, :, None] == expert_ids[None, None, :]
    chosen = jnp.sum(routed.astype(jnp.int32), axis=1)
    earlier = (pack_ids[None, :] < pack_ids[:, None]).astype(jnp.int32)
    rank = jnp.dot(earlier, chosen)
    ranked = jnp.where(chosen > 0, rank, -1)
    place_ids = jnp.arange(most, dtype=jnp.int32)
    hits = ranked.T[:, :, None] == place_ids[None, None, :]
    source_token = jnp.sum(jnp.where(hits, pack_ids[None, :, None], 0), axis=1)
    outgoing = normed[source_token.reshape(-1)].reshape(expert_total, most, -1)
    total_rows = expert_total * most
    received = lax.all_to_all(outgoing, "expert", split_axis=0, concat_axis=0, tiled=True)
    work_rows = received.reshape(total_rows, -1)
    gate_whole, up_whole, down_whole = (
        lax.all_gather(gate_weight, "dp", axis=1, tiled=True),
        lax.all_gather(up_weight, "dp", axis=1, tiled=True),
        lax.all_gather(down_weight, "dp", axis=1, tiled=True),
    )
    produced = expert_output(work_rows, gate_whole[0], up_whole[0], down_whole[0])
    produced = produced.astype(jnp.bfloat16)
    out_slots = produced.reshape(expert_total, most, -1)
    returned = lax.all_to_all(out_slots, "expert", split_axis=0, concat_axis=0, tiled=True)
    flat_back = returned.reshape(total_rows, -1)
    copy_rank = jnp.sum(jnp.where(routed, rank[:, None, :], 0), axis=2)
    copy_index = routes * most + copy_rank
    gates = route_weight / jnp.sum(route_weight, axis=1, keepdims=True)
    mixture = jnp.zeros(hidden_state.shape, jnp.float32)
    for route_slot in range(top_total):
        mixture = mixture + gates[:, route_slot : route_slot + 1] * flat_back[
            copy_index[:, route_slot]
        ].astype(jnp.float32)
    return (hidden_state + mixture).astype(jnp.bfloat16)


def solution(mesh):
    placed = (
        P(("dp", "expert"), None),
        P(("dp", "expert"), None),
        P(("dp", "expert"), None),
        P(("dp", "expert"), None),
        P(("dp", "expert"), None),
        P(("dp", "expert"), None),
        P(("dp", "expert"), None),
        P(),
        P(),
        P("expert", None),
        P(),
        P(("dp", "expert"), None),
        P(("dp", "expert"), None),
        P("expert", "dp", None),
        P("expert", "dp", None),
        P("expert", "dp", None),
    )
    return jax.shard_map(
        local, mesh=mesh, in_specs=placed, out_specs=P(("dp", "expert"), None), check_vma=False
    )
```

profile of v0, /device:TPU:32, one launch (start us, length us, event | category | flops | bytes accessed | tf_op | source)
XLA Modules:
  0.0 508.2 jit_solution(4077008279144218235)
XLA Ops:
  7.4 0.7 all-gather.5.cloned.1.call-update
  8.1 0.8 reduce-window_clone.1
  8.9 0.7 subtract_bitcast_fusion
  9.6 0.8 select_reduce_fusion.4
  10.4 0.7 compare_select_fusion.1
  11.1 4.3 all-to-all-start.1
  15.6 0.7 convert_reduce_fusion
  18.4 2.0 gather_fusion.6
  20.4 1.6 gather_fusion.4
  22.1 1.6 gather_fusion.2
  23.7 1.8 gather_fusion
  25.5 4.9 all-to-all-start.3
  32.0 4.3 all-to-all-done.3
  36.2 3.4 all-to-all-start.2
  39.6 5.7 %all-to-all-done.2 = bf16[8,24,256]{2,1,0:T(8,128)(2,1)S(1)} async-done(((bf16[8,24,256]{2,1,0:T(8,128)(2,1)}), bf16[8,24,256]{2,1,0:T(8,128)(2,1)S(1)}, u32[]{:S(2)}, u32[]{:S(2)}) %all-to-all-start.2) | async-done | bytes 98336 | tf_op jit(solution)/shard_map/all_to_all | solution.py:137
  45.3 3.5 all-to-all-start
  49.1 0.8 gather_fusion.5
  50.1 0.8 gather_fusion.3
  51.0 0.7 copy.56
  51.8 5.8 %all-to-all-done = bf16[8,24,1024]{2,1,0:T(8,128)(2,1)S(1)} async-done(((bf16[8,24,1024]{2,1,0:T(8,128)(2,1)}), bf16[8,24,1024]{2,1,0:T(8,128)(2,1)S(1)}, u32[]{:S(2)}, u32[]{:S(2)}) %all-to-all-start) | async-done | bytes 393248 | tf_op jit(solution)/shard_map/all_to_all | solution.py:144
  57.6 3.5 all-to-all-start.4
  61.4 0.9 gather_fusion.1
  62.3 11.9 %all-to-all-done.4 = bf16[8,24,2048]{2,1,0:T(8,128)(2,1)S(1)} async-done(((bf16[8,24,2048]{2,1,0:T(8,128)(2,1)}), bf16[8,24,2048]{2,1,0:T(8,128)(2,1)S(1)}, u32[]{:S(2)}, u32[]{:S(2)}) %all-to-all-start.4) | async-done | bytes 786464 | tf_op jit(solution)/shard_map/all_to_all | solution.py:123
  74.2 0.9 gather_fusion.7
  77.8 1.4 fusion.11
  79.7 81.6 %all-gather.5.cloned.1.call-done = bf16[2048,1024]{1,0:T(8,128)(2,1)} async-done(((bf16[32,1024]{1,0:T(8,128)(2,1)}), bf16[2048,1024]{1,0:T(8,128)(2,1)}) %all-gather.5.cloned.1.call-update) | async-done | bytes 4194320 | tf_op jit(solution)/shard_map/all_gather | solution.py:66
  161.3 3.0 multiply_reduce_fusion.1
  164.3 0.8 copy-done.4
  165.2 4.3 gather_fusion.8
  169.5 2.3 reshape.331
  171.9 9.3 %all-to-all-start.5 = ((bf16[64,20,1024]{2,1,0:T(8,128)(2,1)}), bf16[64,20,1024]{2,1,0:T(8,128)(2,1)}, u32[]{:S(2)}, u32[]{:S(2)}) async-start(bf16[64,20,1024]{2,1,0:T(8,128)(2,1)} %reshape.331), calls=%async_computation.5 | async-start | bytes 6291456 | tf_op jit(solution)/shard_map/all_to_all | solution.py:177
  182.9 131.6 %all-to-all-done.5 = bf16[64,20,1024]{2,1,0:T(8,128)(2,1)} async-done(((bf16[64,20,1024]{2,1,0:T(8,128)(2,1)}), bf16[64,20,1024]{2,1,0:T(8,128)(2,1)}, u32[]{:S(2)}, u32[]{:S(2)}) %all-to-all-start.5) | async-done | bytes 2621472 | tf_op jit(solution)/shard_map/all_to_all | solution.py:177
  314.6 3.6 reshape.332
  318.3 5.5 %fusion.4 = f32[1280,768]{1,0:T(8,128)} fusion(bf16[1280,1024]{1,0:T(8,128)(2,1)S(1)} %reshape.332, bf16[1,768,1024]{2,1,0:T(8,128)(2,1)} %all-gather.7.cloned.1.call-done), kind=kOutput, calls=%fused_computation.23 | convolution fusion | flops 2013265920 | bytes 8126464 | tf_op jit(solution)/shard_map/dot_general | solution.py:73
  323.8 10.0 %convolution_convert_fusion = bf16[1280,1024]{1,0:T(8,128)(2,1)} fusion(bf16[1,768,1024]{2,1,0:T(8,128)(2,1)} %all-gather.11.cloned.1.call-done, bf16[1280,1024]{1,0:T(8,128)(2,1)S(1)} %reshape.332, f32[1280,768]{1,0:T(8,128)} %fusion.4, bf16[1,768,1024]{2,1,0:T(8,128)(2,1)} %all-gather.9.cloned.1.call-done), kind=kOutput, calls=%fused_computation.19 | convolution fusion | flops 4033740800 | bytes 12320768 | tf_op jit(solution)/shard_map/dot_general | solution.py:76
  333.8 5.2 %reshape.333 = bf16[64,20,1024]{2,1,0:T(8,128)(2,1)} reshape(bf16[1280,1024]{1,0:T(8,128)(2,1)} %convolution_convert_fusion) | data formatting | bytes 5242880 | tf_op jit(solution)/shard_map/reshape | solution.py:186
  339.0 8.0 %all-to-all-start.6 = ((bf16[64,20,1024]{2,1,0:T(8,128)(2,1)}), bf16[64,20,1024]{2,1,0:T(8,128)(2,1)}, u32[]{:S(2)}, u32[]{:S(2)}) async-start(bf16[64,20,1024]{2,1,0:T(8,128)(2,1)} %reshape.333), calls=%async_computation.6 | async-start | bytes 6291456 | tf_op jit(solution)/shard_map/all_to_all | solution.py:187
  347.2 135.2 %all-to-all-done.6 = bf16[64,20,1024]{2,1,0:T(8,128)(2,1)} async-done(((bf16[64,20,1024]{2,1,0:T(8,128)(2,1)}), bf16[64,20,1024]{2,1,0:T(8,128)(2,1)}, u32[]{:S(2)}, u32[]{:S(2)}) %all-to-all-start.6) | async-done | bytes 2621472 | tf_op jit(solution)/shard_map/all_to_all | solution.py:187
  482.4 3.6 reshape.334
  486.1 0.9 gather_fusion.10
  486.9 1.6 gather_fusion.11
  488.5 1.6 gather_fusion.12
  490.1 1.6 gather_fusion.13
  491.6 1.5 gather_fusion.14
  493.2 1.6 gather_fusion.15
  494.7 1.6 gather_fusion.9
  496.3 1.6 gather_fusion.16
  497.9 2.8 add_convert_fusion.1
  (93 shorter events, 9.5 us)
Async XLA Ops:
  7.4 11.0 %copy-start = (bf16[128,2048]{1,0:T(8,128)(2,1)S(1)}, bf16[128,2048]{1,0:T(8,128)(2,1)}, u32[]{:S(2)}) copy-start(bf16[128,2048]{1,0:T(8,128)(2,1)} %param.16) | copy-start | bytes 1572868
  7.4 153.9 %all-gather.5.cloned.1.call-start = ((), (), s32[]{:S(2)}) async-start(), calls=%async_computation.7 | async-start | bytes 4259840 | tf_op jit(solution)/shard_map/all_gather | solution.py:66
  11.1 14.4 %all-to-all-start.1 = ((s32[8,1,24]{2,1,0:T(1,128)}), s32[8,1,24]{2,1,0:T(1,128)S(1)}, u32[]{:S(2)}, u32[]{:S(2)}) async-start(s32[8,1,24]{2,1,0:T(1,128)} %compare_select_fusion.1), calls=%async_computation.1 | async-start | bytes 8192 | tf_op jit(solution)/shard_map/all_to_all | solution.py:151
  16.5 0.6 copy-start.5
  18.4 2.0 copy-start.2
  18.4 3.7 copy-start.3
  20.4 3.3 copy-start.1
  25.5 35.7 %copy-start.14 = (f32[128]{0:T(128)S(1)}, f32[128]{0:T(128)}, u32[]{:S(2)}) copy-start(f32[128]{0:T(128)} %param.24) | copy-start | bytes 1540
  25.5 10.7 %all-to-all-start.3 = ((bf16[8,24,256]{2,1,0:T(8,128)(2,1)}), bf16[8,24,256]{2,1,0:T(8,128)(2,1)S(1)}, u32[]{:S(2)}, u32[]{:S(2)}) async-start(bf16[8,24,256]{2,1,0:T(8,128)(2,1)} %bitcast.14), calls=%async_computation.3 | async-start | bytes 196608 | tf_op jit(solution)/shard_map/all_to_all | solution.py:130
  36.2 9.1 %all-to-all-start.2 = ((bf16[8,24,256]{2,1,0:T(8,128)(2,1)}), bf16[8,24,256]{2,1,0:T(8,128)(2,1)S(1)}, u32[]{:S(2)}, u32[]{:S(2)}) async-start(bf16[8,24,256]{2,1,0:T(8,128)(2,1)} %bitcast.9), calls=%async_computation.2 | async-start | bytes 196608 | tf_op jit(solution)/shard_map/all_to_all | solution.py:137
  45.3 12.3 %all-to-all-start = ((bf16[8,24,1024]{2,1,0:T(8,128)(2,1)}), bf16[8,24,1024]{2,1,0:T(8,128)(2,1)S(1)}, u32[]{:S(2)}, u32[]{:S(2)}) async-start(bf16[8,24,1024]{2,1,0:T(8,128)(2,1)} %bitcast.3), calls=%async_computation | async-start | bytes 786432 | tf_op jit(solution)/shard_map/all_to_all | solution.py:144
  57.6 16.6 %all-to-all-start.4 = ((bf16[8,24,2048]{2,1,0:T(8,128)(2,1)}), bf16[8,24,2048]{2,1,0:T(8,128)(2,1)S(1)}, u32[]{:S(2)}, u32[]{:S(2)}) async-start(bf16[8,24,2048]{2,1,0:T(8,128)(2,1)} %bitcast.19), calls=%async_computation.4 | async-start | bytes 1572864 | tf_op jit(solution)/shard_map/all_to_all | solution.py:123
  61.4 15.8 %copy-start.7 = (bf16[128,2,64]{2,0,1:T(8,128)(2,1)}, bf16[128,2,64]{2,0,1:T(8,128)(2,1)S(1)}, u32[]{:S(2)}) copy-start(bf16[128,2,64]{2,0,1:T(8,128)(2,1)S(1)} %get-tuple-element.12) | copy-start | bytes 98308
  61.4 15.8 %copy-start.8 = (bf16[128,2,64]{2,0,1:T(8,128)(2,1)}, bf16[128,2,64]{2,0,1:T(8,128)(2,1)S(1)}, u32[]{:S(2)}) copy-start(bf16[128,2,64]{2,0,1:T(8,128)(2,1)S(1)} %get-tuple-element.13) | copy-start | bytes 98308
  75.1 0.8 copy-start.15
  77.2 2.0 copy-start.9
  161.3 3.8 copy-start.13
  161.3 3.9 copy-start.11
  164.3 0.8 copy-start.4
  171.9 142.7 %all-to-all-start.5 = ((bf16[64,20,1024]{2,1,0:T(8,128)(2,1)}), bf16[64,20,1024]{2,1,0:T(8,128)(2,1)}, u32[]{:S(2)}, u32[]{:S(2)}) async-start(bf16[64,20,1024]{2,1,0:T(8,128)(2,1)} %reshape.331), calls=%async_computation.5 | async-start | bytes 6291456 | tf_op jit(solution)/shard_map/all_to_all | solution.py:177
  181.2 137.1 %all-gather.7.cloned.1.call-start = ((), (), s32[]{:S(2)}) async-start(), calls=%async_computation.8 | async-start | bytes 1769472 | tf_op jit(solution)/shard_map/all_gather | solution.py:180
  181.8 142.0 %all-gather.11.cloned.1.call-start = ((), (), s32[]{:S(2)}) async-start(), calls=%async_computation.10 | async-start | bytes 1769472 | tf_op jit(solution)/shard_map/all_gather | solution.py:182
  182.4 141.4 %all-gather.9.cloned.1.call-start = ((), (), s32[]{:S(2)}) async-start(), calls=%async_computation.9 | async-start | bytes 1769472 | tf_op jit(solution)/shard_map/all_gather | solution.py:181
  339.0 8.0 %copy-start.12 = (f32[128,8]{0,1:T(8,128)S(1)}, f32[128,8]{0,1:T(8,128)}, u32[]{:S(2)}) copy-start(f32[128,8]{0,1:T(8,128)} %param.28) | copy-start | bytes 12292
  339.0 8.1 %copy-start.6 = (s32[128,64]{0,1:T(8,128)S(1)}, s32[128,64]{0,1:T(8,128)}, u32[]{:S(2)}) copy-start(s32[128,64]{0,1:T(8,128)} %copy-done.5) | copy-start | bytes 98308
  339.0 8.1 %copy-start.10 = (s32[128,8]{0,1:T(8,128)S(1)}, s32[128,8]{0,1:T(8,128)}, u32[]{:S(2)}) copy-start(s32[128,8]{0,1:T(8,128)} %param.27) | copy-start | bytes 12292
  339.0 143.5 %all-to-all-start.6 = ((bf16[64,20,1024]{2,1,0:T(8,128)(2,1)}), bf16[64,20,1024]{2,1,0:T(8,128)(2,1)}, u32[]{:S(2)}, u32[]{:S(2)}) async-start(bf16[64,20,1024]{2,1,0:T(8,128)(2,1)} %reshape.333), calls=%async_computation.6 | async-start | bytes 6291456 | tf_op jit(solution)/shard_map/all_to_all | solution.py:187
Sparse Core Ops, SparseCore 0:
  11.1 150.1 all-gather.4
Sparse Core Ops, SparseCore 1:
  183.8 32.6 all-gather.6
  218.4 32.1 all-gather.10
  252.6 32.1 all-gather.8
where the time goes:
time: 509 us; the launch traced here: 508 us
  waiting for transfers between devices  379 us (74%)
  local copies, waits for them, and re-layouts  45.3 us (9%)
  starting transfers between devices  37.1 us (7%)
  matrix products  21.2 us (4%)
  between operations  15.5 us (3%)
  other arithmetic  10.6 us (2%)
    all_to_all x1, waiting for transfers between devices, local(): lax.all_to_all(out_slots, 'expert', split_axis=0, concat_axis=0, tiled=True)  135 us
    all_to_all x1, waiting for transfers between devices, local(): lax.all_to_all(outgoing, 'expert', split_axis=0, concat_axis=0, tiled=True)  132 us
    all_gather x1, waiting for transfers between devices, project_heads(): lax.all_gather(output_weight, 'expert', axis=0, tiled=True)  81.6 us
    all_to_all x1, waiting for transfers between devices, local(): lax.all_to_all(query_rows[source_rows].reshape(owner_total, capacity, -1)...  11.9 us
    gather x8, local copies, waits for them, and re-layouts, local(): flat_back[copy_index[:, route_slot]].astype(jnp.float32)  11.8 us
  transfers between devices with their start and end apart: 11, of which 7 were waited for; matrix products, arithmetic and copies ran while one was open for 6% of the time, Pallas kernels for 0%

commit v1 on v0

--- a/solution.py
+++ b/solution.py
@@ -63,7 +63,12 @@
 def project_heads(attended, output_weight):
     return jnp.dot(
         attended,
-        lax.all_gather(output_weight, "expert", axis=0, tiled=True),
+        jnp.concatenate(
+            lax.all_to_all(
+                jnp.stack([output_weight for _ in range(lax.axis_size("expert"))]), "expert", 0, 0
+            ),
+            axis=0,
+        ),
         preferred_element_type=jnp.float32,
     )
 

time: 509 us -> 636 us (1.25)
  waiting for transfers between devices: 379 us -> 477 us
  blocking collectives: 0 us -> 15.6 us
  starting transfers between devices: 37.1 us -> 49.5 us
    all_to_all x1, waiting for transfers between devices: 11.9 us -> 174 us  [project_heads(): lax.all_to_all(jnp.stack([output_weight for _ in range(lax.axis_size('exp...]
    all_gather x1 -> x0, waiting for transfers between devices: 81.6 us -> none  [project_heads(): lax.all_gather(output_weight, 'expert', axis=0, tiled=True)]
    all_to_all x0 -> x1, blocking collectives: none -> 15.6 us  [local(): lax.all_to_all(query_rows[source_rows].reshape(owner_total, capacity, -1)...]
    all_to_all x1, starting transfers between devices: 3.55 us -> 18.7 us  [project_heads(): lax.all_to_all(jnp.stack([output_weight for _ in range(lax.axis_size('exp...]
    all_to_all x1, waiting for transfers between devices: 132 us -> 140 us  [local(): lax.all_to_all(outgoing, 'expert', split_axis=0, concat_axis=0, tiled=True)]
    all_to_all x1, waiting for transfers between devices: 135 us -> 143 us  [local(): lax.all_to_all(out_slots, 'expert', split_axis=0, concat_axis=0, tiled=True)]
  transfers between devices with their start and end apart: 11 -> 10, of which waited for: 7 -> 7; matrix products, arithmetic and copies ran while one was open for 6% -> 5% of each run, Pallas kernels for 0% -> 0%
where the time goes in v1:
time: 636 us; the launch traced here: 635 us
  waiting for transfers between devices  477 us (75%)
  starting transfers between devices  49.5 us (8%)
  local copies, waits for them, and re-layouts  48.4 us (8%)
  matrix products  21.2 us (3%)
  blocking collectives  15.6 us (2%)
  between operations  13.6 us (2%)
  other arithmetic  10 us (2%)
    all_to_all x1, waiting for transfers between devices, project_heads(): lax.all_to_all(jnp.stack([output_weight for _ in range(lax.axis_size('exp...  174 us
    all_to_all x1, waiting for transfers between devices, local(): lax.all_to_all(out_slots, 'expert', split_axis=0, concat_axis=0, tiled=True)  143 us
    all_to_all x1, waiting for transfers between devices, local(): lax.all_to_all(outgoing, 'expert', split_axis=0, concat_axis=0, tiled=True)  140 us
    all_to_all x1, starting transfers between devices, project_heads(): lax.all_to_all(jnp.stack([output_weight for _ in range(lax.axis_size('exp...  18.7 us
    all_to_all x1, blocking collectives, local(): lax.all_to_all(query_rows[source_rows].reshape(owner_total, capacity, -1)...  15.6 us
  transfers between devices with their start and end apart: 10, of which 7 were waited for; matrix products, arithmetic and copies ran while one was open for 5% of the time, Pallas kernels for 0%

profile of v1, /device:TPU:32, one launch (start us, length us, event | category | flops | bytes accessed | tf_op | source)
XLA Modules:
  0.0 634.8 jit_solution(3405658623122743623)
XLA Ops:
  6.5 0.9 reduce-window_clone.1
  8.1 0.8 select_reduce_fusion.4
  8.9 0.7 compare_select_fusion.1
  9.6 4.3 all-to-all-start.1
  14.1 2.3 gather_fusion.4
  16.4 2.7 all-to-all-done.1
  19.1 3.4 all-to-all-start.3
  22.5 2.4 gather_fusion.2
  24.9 3.4 all-to-all-done.3
  28.2 3.4 all-to-all-start.2
  31.6 1.7 gather_fusion
  33.4 4.0 all-to-all-done.2
  37.3 3.5 all-to-all-start
  40.8 1.1 gather_fusion.6
  41.9 7.7 %all-to-all-done = bf16[8,24,1024]{2,1,0:T(8,128)(2,1)S(1)} async-done(((bf16[8,24,1024]{2,1,0:T(8,128)(2,1)}), bf16[8,24,1024]{2,1,0:T(8,128)(2,1)S(1)}, u32[]{:S(2)}, u32[]{:S(2)}) %all-to-all-start) | async-done | bytes 393248 | tf_op jit(solution)/shard_map/all_to_all | solution.py:149
  49.6 15.6 %all_to_all.41 = bf16[8,24,2048]{2,1,0:T(8,128)(2,1)S(1)} all-to-all(bf16[8,24,2048]{2,1,0:T(8,128)(2,1)S(1)} %bitcast.109), channel_id=1, replica_groups=mesh['dp'=8,'expert'=64] {'dp'}, dimensions={0} | all-to-all | bytes 1572864 | tf_op jit(solution)/shard_map/all_to_all | solution.py:128
  65.2 2.5 stack.2
  67.7 18.7 %all-to-all-start.5 = ((bf16[64,32,1024]{2,1,0:T(8,128)(2,1)}), bf16[64,32,1024]{2,1,0:T(8,128)(2,1)}, u32[]{:S(2)}, u32[]{:S(2)}) async-start(bf16[64,32,1024]{2,1,0:T(8,128)(2,1)} %stack.2), calls=%async_computation.5 | async-start | bytes 8388608 | tf_op jit(solution)/shard_map/all_to_all | solution.py:67
  90.4 0.8 gather_fusion.5
  91.4 0.8 gather_fusion.3
  92.3 0.7 copy.56
  93.3 0.9 gather_fusion.1
  94.2 0.9 gather_fusion.7
  97.8 1.4 fusion.11
  99.6 173.7 %all-to-all-done.5 = bf16[64,32,1024]{2,1,0:T(8,128)(2,1)} async-done(((bf16[64,32,1024]{2,1,0:T(8,128)(2,1)}), bf16[64,32,1024]{2,1,0:T(8,128)(2,1)}, u32[]{:S(2)}, u32[]{:S(2)}) %all-to-all-start.5) | async-done | bytes 4194336 | tf_op jit(solution)/shard_map/all_to_all | solution.py:67
  273.3 3.0 multiply_reduce_fusion.1
  276.4 0.8 copy-done.2
  277.3 4.3 gather_fusion.8
  281.6 2.4 reshape.337
  284.0 8.3 %all-to-all-start.6 = ((bf16[64,20,1024]{2,1,0:T(8,128)(2,1)}), bf16[64,20,1024]{2,1,0:T(8,128)(2,1)}, u32[]{:S(2)}, u32[]{:S(2)}) async-start(bf16[64,20,1024]{2,1,0:T(8,128)(2,1)} %reshape.337), calls=%async_computation.6 | async-start | bytes 6291456 | tf_op jit(solution)/shard_map/all_to_all | solution.py:182
  293.1 0.7 all-gather.6.cloned.1.call-update
  294.5 140.4 %all-to-all-done.6 = bf16[64,20,1024]{2,1,0:T(8,128)(2,1)} async-done(((bf16[64,20,1024]{2,1,0:T(8,128)(2,1)}), bf16[64,20,1024]{2,1,0:T(8,128)(2,1)}, u32[]{:S(2)}, u32[]{:S(2)}) %all-to-all-start.6) | async-done | bytes 2621472 | tf_op jit(solution)/shard_map/all_to_all | solution.py:182
  434.9 3.6 reshape.338
  438.6 5.5 fusion.4
  444.1 10.0 %convolution_convert_fusion = bf16[1280,1024]{1,0:T(8,128)(2,1)} fusion(bf16[1,768,1024]{2,1,0:T(8,128)(2,1)} %all-gather.8.cloned.1.call-done, bf16[1280,1024]{1,0:T(8,128)(2,1)S(1)} %reshape.338, f32[1280,768]{1,0:T(8,128)} %fusion.4, bf16[1,768,1024]{2,1,0:T(8,128)(2,1)} %all-gather.6.cloned.1.call-done), kind=kOutput, calls=%fused_computation.19 | convolution fusion | flops 4033740800 | bytes 12320768 | tf_op jit(solution)/shard_map/dot_general | solution.py:81
  454.1 5.2 reshape.339
  459.3 7.9 %all-to-all-start.7 = ((bf16[64,20,1024]{2,1,0:T(8,128)(2,1)}), bf16[64,20,1024]{2,1,0:T(8,128)(2,1)}, u32[]{:S(2)}, u32[]{:S(2)}) async-start(bf16[64,20,1024]{2,1,0:T(8,128)(2,1)} %reshape.339), calls=%async_computation.7 | async-start | bytes 6291456 | tf_op jit(solution)/shard_map/all_to_all | solution.py:192
  467.4 142.7 %all-to-all-done.7 = bf16[64,20,1024]{2,1,0:T(8,128)(2,1)} async-done(((bf16[64,20,1024]{2,1,0:T(8,128)(2,1)}), bf16[64,20,1024]{2,1,0:T(8,128)(2,1)}, u32[]{:S(2)}, u32[]{:S(2)}) %all-to-all-start.7) | async-done | bytes 2621472 | tf_op jit(solution)/shard_map/all_to_all | solution.py:192
  610.1 3.6 reshape.340
  613.7 0.9 gather_fusion.10
  614.6 1.6 gather_fusion.11
  616.1 1.6 gather_fusion.12
  617.7 1.6 gather_fusion.13
  619.3 1.6 gather_fusion.14
  620.8 1.6 gather_fusion.15
  622.4 1.6 gather_fusion.9
  624.0 1.6 gather_fusion.16
  625.5 2.8 add_convert_fusion.1
  (92 shorter events, 10.0 us)
Async XLA Ops:
  6.5 34.2 %copy-start = (bf16[128,2048]{1,0:T(8,128)(2,1)S(1)}, bf16[128,2048]{1,0:T(8,128)(2,1)}, u32[]{:S(2)}) copy-start(bf16[128,2048]{1,0:T(8,128)(2,1)} %param.16) | copy-start | bytes 1572868
  6.5 25.1 %copy-start.1 = (bf16[128,1024]{1,0:T(8,128)(2,1)S(1)}, bf16[128,1024]{1,0:T(8,128)(2,1)}, u32[]{:S(2)}) copy-start(bf16[128,1024]{1,0:T(8,128)(2,1)} %param.19) | copy-start | bytes 786436
  9.6 9.5 %all-to-all-start.1 = ((s32[8,1,24]{2,1,0:T(1,128)}), s32[8,1,24]{2,1,0:T(1,128)S(1)}, u32[]{:S(2)}, u32[]{:S(2)}) async-start(s32[8,1,24]{2,1,0:T(1,128)} %compare_select_fusion.1), calls=%async_computation.1 | async-start | bytes 8192 | tf_op jit(solution)/shard_map/all_to_all | solution.py:156
  19.1 9.1 %all-to-all-start.3 = ((bf16[8,24,256]{2,1,0:T(8,128)(2,1)}), bf16[8,24,256]{2,1,0:T(8,128)(2,1)S(1)}, u32[]{:S(2)}, u32[]{:S(2)}) async-start(bf16[8,24,256]{2,1,0:T(8,128)(2,1)} %bitcast.14), calls=%async_computation.3 | async-start | bytes 196608 | tf_op jit(solution)/shard_map/all_to_all | solution.py:135
  28.2 9.1 %all-to-all-start.2 = ((bf16[8,24,256]{2,1,0:T(8,128)(2,1)}), bf16[8,24,256]{2,1,0:T(8,128)(2,1)S(1)}, u32[]{:S(2)}, u32[]{:S(2)}) async-start(bf16[8,24,256]{2,1,0:T(8,128)(2,1)} %bitcast.9), calls=%async_computation.2 | async-start | bytes 196608 | tf_op jit(solution)/shard_map/all_to_all | solution.py:142
  37.3 12.3 %all-to-all-start = ((bf16[8,24,1024]{2,1,0:T(8,128)(2,1)}), bf16[8,24,1024]{2,1,0:T(8,128)(2,1)S(1)}, u32[]{:S(2)}, u32[]{:S(2)}) async-start(bf16[8,24,1024]{2,1,0:T(8,128)(2,1)} %bitcast.3), calls=%async_computation | async-start | bytes 786432 | tf_op jit(solution)/shard_map/all_to_all | solution.py:149
  40.8 24.4 %copy-start.7 = (bf16[32,1024]{1,0:T(8,128)(2,1)S(1)}, bf16[32,1024]{1,0:T(8,128)(2,1)}, u32[]{:S(2)}) copy-start(bf16[32,1024]{1,0:T(8,128)(2,1)} %param.25) | copy-start | bytes 196612
  67.7 18.7 %copy-start.9 = (s32[128,8]{0,1:T(8,128)S(1)}, s32[128,8]{0,1:T(8,128)}, u32[]{:S(2)}) copy-start(s32[128,8]{0,1:T(8,128)} %param.27) | copy-start | bytes 12292
  67.7 25.4 %copy-start.14 = (f32[128]{0:T(128)S(1)}, f32[128]{0:T(128)}, u32[]{:S(2)}) copy-start(f32[128]{0:T(128)} %param.24) | copy-start | bytes 1540
  67.7 205.6 %all-to-all-start.5 = ((bf16[64,32,1024]{2,1,0:T(8,128)(2,1)}), bf16[64,32,1024]{2,1,0:T(8,128)(2,1)}, u32[]{:S(2)}, u32[]{:S(2)}) async-start(bf16[64,32,1024]{2,1,0:T(8,128)(2,1)} %stack.2), calls=%async_computation.5 | async-start | bytes 8388608 | tf_op jit(solution)/shard_map/all_to_all | solution.py:67
  86.7 0.6 copy-start.3
  93.3 3.9 copy-start.5
  93.3 3.9 copy-start.6
  95.1 0.8 copy-start.15
  97.1 2.0 copy-start.8
  273.3 3.8 copy-start.13
  273.3 4.0 copy-start.11
  276.4 0.8 copy-start.2
  284.0 151.0 %all-to-all-start.6 = ((bf16[64,20,1024]{2,1,0:T(8,128)(2,1)}), bf16[64,20,1024]{2,1,0:T(8,128)(2,1)}, u32[]{:S(2)}, u32[]{:S(2)}) async-start(bf16[64,20,1024]{2,1,0:T(8,128)(2,1)} %reshape.337), calls=%async_computation.6 | async-start | bytes 6291456 | tf_op jit(solution)/shard_map/all_to_all | solution.py:182
  292.3 146.3 %all-gather.4.cloned.1.call-start = ((), (), s32[]{:S(2)}) async-start(), calls=%async_computation.8 | async-start | bytes 1769472 | tf_op jit(solution)/shard_map/all_gather | solution.py:185
  293.0 151.1 %all-gather.6.cloned.1.call-start = ((), (), s32[]{:S(2)}) async-start(), calls=%async_computation.9 | async-start | bytes 1769472 | tf_op jit(solution)/shard_map/all_gather | solution.py:186
  293.8 150.4 %all-gather.8.cloned.1.call-start = ((), (), s32[]{:S(2)}) async-start(), calls=%async_computation.10 | async-start | bytes 1769472 | tf_op jit(solution)/shard_map/all_gather | solution.py:187
  459.3 7.9 %copy-start.12 = (f32[128,8]{0,1:T(8,128)S(1)}, f32[128,8]{0,1:T(8,128)}, u32[]{:S(2)}) copy-start(f32[128,8]{0,1:T(8,128)} %param.28) | copy-start | bytes 12292
  459.3 7.9 %copy-start.4 = (s32[128,64]{0,1:T(8,128)S(1)}, s32[128,64]{0,1:T(8,128)}, u32[]{:S(2)}) copy-start(s32[128,64]{0,1:T(8,128)} %copy-done.3) | copy-start | bytes 98308
  459.3 7.9 %copy-start.10 = (s32[128,8]{0,1:T(8,128)S(1)}, s32[128,8]{0,1:T(8,128)}, u32[]{:S(2)}) copy-start(s32[128,8]{0,1:T(8,128)} %param.27) | copy-start | bytes 12292
  459.3 150.7 %all-to-all-start.7 = ((bf16[64,20,1024]{2,1,0:T(8,128)(2,1)}), bf16[64,20,1024]{2,1,0:T(8,128)(2,1)}, u32[]{:S(2)}, u32[]{:S(2)}) async-start(bf16[64,20,1024]{2,1,0:T(8,128)(2,1)} %reshape.339), calls=%async_computation.7 | async-start | bytes 6291456 | tf_op jit(solution)/shard_map/all_to_all | solution.py:192
Sparse Core Ops, SparseCore 0:
  295.2 30.9 all-gather.3
  328.3 32.2 all-gather.5
  362.7 32.2 all-gather.7
